TPU v7x, 128 devices: a whole 4x4x4 slice. The times are simulated.
128 devices in a mesh: head: 4 (over z), page: 32 (over x, y, core).
Axes of the slice: x: 4, y: 4, z: 4, core: 2. Of those that a mesh axis runs over, the one named last changes fastest.
Arguments:
- hidden_in: bfloat16 [32, 1024, 1024], P('page', 'head'), may hold values from -6 to 6
- norm_gain: float32 [1024], replicated, may hold values from 0.1 to 1.9
- w_qkv: bfloat16 [1024, 3, 1024], P(None, None, 'head'), may hold values from -0.1875 to 0.1875
- w_out: bfloat16 [1024, 1024], P('head'), may hold values from -0.75 to 0.75
- cache_kv: bfloat16 [2, 64, 128, 1024], P(None, 'page', None, 'head'), may hold values from -110 to 110, as said below
- page_node: int32 [64], replicated, may hold values from 0 to 18, as said below
- page_fill: int32 [64], replicated, may hold values from 1 to 128
- node_parent: int32 [19], replicated, may hold values from 0 to 2, as said below
- tok_seg: int32 [32, 1024], P('page'), may hold values from 0 to 7, never falling along the last dimension, each value on 1 to 256 neighbouring positions
- req_leaf: int32 [32, 8], P('page'), may hold values from 3 to 18, as said below
Outputs:
- attn_out: bfloat16 [32, 1024, 1024], P('page', 'head')
Inputs may be any that keep to these rules, and one draw needn't show every extreme that they name: `cache_kv`: entries of the cache; keys and values. `page_node`: every node owns at least one page. `node_parent`: node 0 is the root and its own parent; nodes 1 to 2 have parent 0; the others have a parent among nodes 1 to 2, and each of those has a child. `req_leaf`: each request names a lowest-level node; every lowest-level node is named by some request.
All inputs are finite; a program needn't handle non-finite values.
Results may differ from a plain program's by a relative error of at most 0.018.
Values may be sent and summed in bfloat16 or wider, within the bound.
No kernel may reach another device: no remote copies, remote signals or barrier semaphores. Data moves between devices by JAX's collectives and lax.ppermute only.
A program may use at most 64 MiB of HBM per device.

v0:
```python
import math
import jax
import jax.numpy as jnp
from jax import lax
from jax.sharding import PartitionSpec as P

HD = 64
EPSILON = 1e-06
FLOOR_SCORE = -1e30


def lookup(indices, lookup_table):
    matches = indices[:, None] == jnp.arange(lookup_table.shape[0], dtype=jnp.int32)[None, :]
    return jnp.sum(jnp.where(matches, lookup_table[None, :], 0), axis=1)


def shards(
    hidden_in,
    norm_gain,
    w_qkv,
    w_out,
    cache_kv,
    page_node,
    page_fill,
    node_parent,
    tok_seg,
    req_leaf,
):
    widened = hidden_in[0].astype(jnp.float32)
    normed = (
        widened
        * lax.rsqrt(jnp.mean(widened * widened, axis=1, keepdims=True) + EPSILON)
        * norm_gain
    ).astype(jnp.bfloat16)
    model_width = widened.shape[1]
    group_width = w_qkv.shape[2]
    head_size = HD
    group_heads = group_width // head_size
    weight_flat = w_qkv.reshape(model_width, 3 * group_width)
    projected = jnp.dot(
        lax.all_gather(normed, "head", axis=0, tiled=True),
        weight_flat,
        preferred_element_type=jnp.float32,
    ).astype(jnp.bfloat16)
    queries_all = projected.shape[0]
    queries = projected[:, :group_width].reshape(queries_all, group_heads, head_size)
    key_new = projected[:, group_width : 2 * group_width].reshape(
        queries_all, group_heads, head_size
    )
    value_new = projected[:, 2 * group_width :].reshape(queries_all, group_heads, head_size)
    score_scale = head_size ** (-0.5)
    segment = tok_seg[0]
    leaf_node = lookup(segment, req_leaf[0])
    upper_node = lookup(leaf_node, node_parent)
    root_node = lookup(upper_node, node_parent)
    position = jnp.arange(queries_all, dtype=jnp.int32)
    block_rows = min(queries_all, 512)

    def suffix_block(first):
        query_rows = lax.dynamic_slice_in_dim(queries, first, block_rows, 0)
        segment_rows = lax.dynamic_slice_in_dim(segment, first, block_rows, 0)
        position_rows = first + jnp.arange(block_rows, dtype=jnp.int32)
        visible = (segment_rows[:, None] == segment[None, :]) & (
            position[None, :] <= position_rows[:, None]
        )
        scores = (
            jnp.einsum("qhd,khd->hqk", query_rows, key_new, preferred_element_type=jnp.float32)
            * score_scale
        )
        scores = jnp.where(visible[None], scores, FLOOR_SCORE)
        row_max = jnp.max(scores, axis=2)
        weights = jnp.where(visible[None], jnp.exp(scores - row_max[:, :, None]), 0.0)
        row_sum = jnp.sum(weights, axis=2)
        weighted = jnp.einsum(
            "hqk,khd->hqd",
            weights.astype(jnp.bfloat16),
            value_new,
            preferred_element_type=jnp.float32,
        )
        return (row_max, row_sum, weighted)

    block_starts = jnp.arange(0, queries_all, block_rows, dtype=jnp.int32)
    block_max, block_sum, block_weighted = lax.map(suffix_block, block_starts)
    initial = (
        jnp.transpose(block_max, (1, 0, 2)).reshape(group_heads, queries_all),
        jnp.transpose(block_sum, (1, 0, 2)).reshape(group_heads, queries_all),
        jnp.transpose(block_weighted, (1, 0, 2, 3)).reshape(group_heads, queries_all, head_size),
    )
    page_len = cache_kv.shape[2]
    page_slot = jnp.arange(page_len, dtype=jnp.int32)
    shard_piece = lax.all_gather(cache_kv, "page", axis=1, tiled=True)
    piece_pages = shard_piece.shape[1]
    group_pages = math.gcd(piece_pages, 4)
    step_count = piece_pages // group_pages
    block_keys = group_pages * page_len
    key_blocks = shard_piece[0].reshape(step_count, block_keys, group_heads, head_size)
    value_blocks = shard_piece[1].reshape(step_count, block_keys, group_heads, head_size)
    key_nodes = jnp.repeat(page_node, page_len).reshape(step_count, block_keys)
    key_valid = (page_slot[None, :] < page_fill[:, None]).reshape(step_count, block_keys)

    def one_step(partial_value, inputs):
        row_max, row_sum, weighted = partial_value
        key_block, value_block, node_block, valid_block = inputs
        visible = (
            (node_block[None, :] == leaf_node[:, None])
            | (node_block[None, :] == upper_node[:, None])
            | (node_block[None, :] == root_node[:, None])
        ) & valid_block[None, :]
        scores = (
            jnp.einsum("qhd,khd->hqk", queries, key_block, preferred_element_type=jnp.float32)
            * score_scale
        )
        scores = jnp.where(visible[None], scores, FLOOR_SCORE)
        new_max = jnp.maximum(row_max, jnp.max(scores, axis=2))
        rescale = jnp.exp(row_max - new_max)
        weights = jnp.where(visible[None], jnp.exp(scores - new_max[:, :, None]), 0.0)
        row_sum = row_sum * rescale + jnp.sum(weights, axis=2)
        weighted = weighted * rescale[:, :, None] + jnp.einsum(
            "hqk,khd->hqd",
            weights.astype(jnp.bfloat16),
            value_block,
            preferred_element_type=jnp.float32,
        )
        return ((new_max, row_sum, weighted), None)

    result_state, unused = lax.scan(
        one_step, initial, (key_blocks, value_blocks, key_nodes, key_valid)
    )
    final_max, final_sum, final_weighted = result_state
    attention = (final_weighted / final_sum[:, :, None]).astype(jnp.bfloat16)
    attention = jnp.transpose(attention, (1, 0, 2)).reshape(queries_all, group_width)
    result = lax.psum_scatter(
        jnp.dot(attention, w_out, preferred_element_type=jnp.float32).astype(jnp.bfloat16),
        "head",
        scatter_dimension=0,
        tiled=True,
    )
    return result[None]


def solution(mesh):
    placed = (
        P("page", "head", None),
        P(),
        P(None, None, "head"),
        P("head", None),
        P(None, "page", None, "head"),
        P(),
        P(),
        P(),
        P("page", None),
        P("page", None),
    )
    return jax.shard_map(
        shards, mesh=mesh, in_specs=placed, out_specs=P("page", "head", None), check_vma=False
    )
```

profile of v0, /device:TPU:1, one launch (start us, length us, event | category | flops | bytes accessed | tf_op | source)
XLA Modules:
  0.0 339.6 jit_solution(15440758614901769843)
XLA Ops:
  16.4 27.6 %all-gather.3.cloned.1.call-done = bf16[1024,1024]{1,0:T(8,128)(2,1)} async-done(((bf16[256,1024]{1,0:T(8,128)(2,1)}), bf16[1024,1024]{1,0:T(8,128)(2,1)}) %all-gather.3.cloned.1.call-update) | async-done | bytes 2097168 | tf_op jit(solution)/shard_map/all_gather | solution.py:41
  48.4 24.0 %while.30 = (s32[]{:T(128)}, f32[2,4,512]{2,1,0:T(4,128)S(1)}, f32[2,4,512]{2,1,0:T(4,128)S(1)}, f32[2,4,512,64]{2,3,1,0:T(8,128)S(1)}, s32[2]{0:T(128)S(1)}, /*...) while((s32[]{:T(128)}, f32[2,4,512]{2,1,0:T(4,128)S(1)}, ...), condition=%wide.region_4.5_spmd.clone, body=%wide.region_1.4_spmd.clone.sunk | while | flops 565703168 | bytes 29178048 | solution.py:83
  72.5 27.1 %all-gather.5.cloned.1.call-done = bf16[2,64,128,256]{3,2,1,0:T(8,128)(2,1)} async-done(((bf16[2,2,128,256]{3,2,1,0:T(8,128)(2,1)}), bf16[2,64,128,256]{3,2,1,0:T(8,128)(2,1)}) %all-gather.5.cloned.1.call-update) | async-done | bytes 8388624 | tf_op jit(solution)/shard_map/all_gather | solution.py:91
  99.5 6.0 %fusion.43 = (bf16[1,64,128,256]{3,2,1,0:T(8,128)(2,1)}, bf16[1,64,128,256]{3,2,1,0:T(8,128)(2,1)}) fusion(bf16[2,64,128,256]{3,2,1,0:T(8,128)(2,1)} %all-gather.5.cloned.1.call-done), kind=kLoop, calls=%fused_computation.63 | loop fusion | bytes 16777216 | tf_op jit(solution)/shard_map/slice | solution.py:97
  105.5 12.9 %reshape.224 = bf16[16,512,4,64]{3,2,1,0:T(4,128)(2,1)} reshape(bf16[1,64,128,256]{3,2,1,0:T(8,128)(2,1)} %get-tuple-element.231) | data formatting | bytes 8388608 | tf_op jit(solution)/shard_map/reshape;squeeze | solution.py:96
  118.4 12.7 %copy.24 = bf16[16,512,4,64]{1,3,2,0:T(8,128)(2,1)} copy(bf16[16,512,4,64]{3,2,1,0:T(4,128)(2,1)} %reshape.224) | data formatting | bytes 8388608 | tf_op jit(solution)/shard_map/while | solution.py:126
  131.1 12.9 %reshape.225 = bf16[16,512,4,64]{3,2,1,0:T(4,128)(2,1)} reshape(bf16[1,64,128,256]{3,2,1,0:T(8,128)(2,1)} %get-tuple-element.230) | data formatting | bytes 8388608 | tf_op jit(solution)/shard_map/reshape;squeeze | solution.py:97
  144.0 12.7 %copy.25 = bf16[16,512,4,64]{1,3,2,0:T(8,128)(2,1)} copy(bf16[16,512,4,64]{3,2,1,0:T(4,128)(2,1)} %reshape.225) | data formatting | bytes 8388608 | tf_op jit(solution)/shard_map/while | solution.py:126
  156.7 145.0 %while.29 = (s32[]{:T(128)}, f32[4,1024]{1,0:T(4,128)S(1)}, f32[4,1024]{1,0:T(4,128)S(1)}, f32[4,1024,64]{1,2,0:T(8,128)S(1)}, s32[16,512]{1,0:T(8,128)S(1)}, /*...) while((s32[]{:T(128)}, f32[4,1024]{1,0:T(4,128)S(1)}, ...), condition=%wide.region_11.12_spmd, body=%wide.region_8.11_spmd.sunk | while | flops 567812096 | bytes 30691972 | solution.py:126
  162.0 3.6 %fusion.70 = f32[4,1024,64]{1,2,0:T(8,128)S(1)} fusion(f32[4,512,1024]{2,1,0:T(8,128)S(1)} %get-tuple-element.368, f32[4,1024]{1,0:T(4,128)S(1)} %max.4, pred[1024,512]{0,1:T(8,128)(4,1)S(1)} %or_and_fusion.2, f32[4,1024,64]{1,2,0:T(8,128)S(1)} %get-tuple-element.440, f32[4,1024]{1,0:T(4,128)S(1)} %get-tuple-element.370, ...), kind=kOutput, calls=%fused_computation.29.clone.1 | convolution fusion | flops 279445504 | bytes 11305472 | tf_op jit(solution)/shard_map/while/body/eval_jaxpr/hqk,khd->hqd/dot_general | solution.py:118
  171.1 3.6 %fusion.70 = f32[4,1024,64]{1,2,0:T(8,128)S(1)} fusion(f32[4,512,1024]{2,1,0:T(8,128)S(1)} %get-tuple-element.368, f32[4,1024]{1,0:T(4,128)S(1)} %max.4, pred[1024,512]{0,1:T(8,128)(4,1)S(1)} %or_and_fusion.2, f32[4,1024,64]{1,2,0:T(8,128)S(1)} %get-tuple-element.440, f32[4,1024]{1,0:T(4,128)S(1)} %get-tuple-element.370, ...), kind=kOutput, calls=%fused_computation.29.clone.1 | convolution fusion | flops 279445504 | bytes 11305472 | tf_op jit(solution)/shard_map/while/body/eval_jaxpr/hqk,khd->hqd/dot_general | solution.py:118
  180.2 3.6 %fusion.70 = f32[4,1024,64]{1,2,0:T(8,128)S(1)} fusion(f32[4,512,1024]{2,1,0:T(8,128)S(1)} %get-tuple-element.368, f32[4,1024]{1,0:T(4,128)S(1)} %max.4, pred[1024,512]{0,1:T(8,128)(4,1)S(1)} %or_and_fusion.2, f32[4,1024,64]{1,2,0:T(8,128)S(1)} %get-tuple-element.440, f32[4,1024]{1,0:T(4,128)S(1)} %get-tuple-element.370, ...), kind=kOutput, calls=%fused_computation.29.clone.1 | convolution fusion | flops 279445504 | bytes 11305472 | tf_op jit(solution)/shard_map/while/body/eval_jaxpr/hqk,khd->hqd/dot_general | solution.py:118
  189.2 3.6 %fusion.70 = f32[4,1024,64]{1,2,0:T(8,128)S(1)} fusion(f32[4,512,1024]{2,1,0:T(8,128)S(1)} %get-tuple-element.368, f32[4,1024]{1,0:T(4,128)S(1)} %max.4, pred[1024,512]{0,1:T(8,128)(4,1)S(1)} %or_and_fusion.2, f32[4,1024,64]{1,2,0:T(8,128)S(1)} %get-tuple-element.440, f32[4,1024]{1,0:T(4,128)S(1)} %get-tuple-element.370, ...), kind=kOutput, calls=%fused_computation.29.clone.1 | convolution fusion | flops 279445504 | bytes 11305472 | tf_op jit(solution)/shard_map/while/body/eval_jaxpr/hqk,khd->hqd/dot_general | solution.py:118
  198.3 3.6 %fusion.70 = f32[4,1024,64]{1,2,0:T(8,128)S(1)} fusion(f32[4,512,1024]{2,1,0:T(8,128)S(1)} %get-tuple-element.368, f32[4,1024]{1,0:T(4,128)S(1)} %max.4, pred[1024,512]{0,1:T(8,128)(4,1)S(1)} %or_and_fusion.2, f32[4,1024,64]{1,2,0:T(8,128)S(1)} %get-tuple-element.440, f32[4,1024]{1,0:T(4,128)S(1)} %get-tuple-element.370, ...), kind=kOutput, calls=%fused_computation.29.clone.1 | convolution fusion | flops 279445504 | bytes 11305472 | tf_op jit(solution)/shard_map/while/body/eval_jaxpr/hqk,khd->hqd/dot_general | solution.py:118
  207.4 3.6 %fusion.70 = f32[4,1024,64]{1,2,0:T(8,128)S(1)} fusion(f32[4,512,1024]{2,1,0:T(8,128)S(1)} %get-tuple-element.368, f32[4,1024]{1,0:T(4,128)S(1)} %max.4, pred[1024,512]{0,1:T(8,128)(4,1)S(1)} %or_and_fusion.2, f32[4,1024,64]{1,2,0:T(8,128)S(1)} %get-tuple-element.440, f32[4,1024]{1,0:T(4,128)S(1)} %get-tuple-element.370, ...), kind=kOutput, calls=%fused_computation.29.clone.1 | convolution fusion | flops 279445504 | bytes 11305472 | tf_op jit(solution)/shard_map/while/body/eval_jaxpr/hqk,khd->hqd/dot_general | solution.py:118
  216.4 3.6 %fusion.70 = f32[4,1024,64]{1,2,0:T(8,128)S(1)} fusion(f32[4,512,1024]{2,1,0:T(8,128)S(1)} %get-tuple-element.368, f32[4,1024]{1,0:T(4,128)S(1)} %max.4, pred[1024,512]{0,1:T(8,128)(4,1)S(1)} %or_and_fusion.2, f32[4,1024,64]{1,2,0:T(8,128)S(1)} %get-tuple-element.440, f32[4,1024]{1,0:T(4,128)S(1)} %get-tuple-element.370, ...), kind=kOutput, calls=%fused_computation.29.clone.1 | convolution fusion | flops 279445504 | bytes 11305472 | tf_op jit(solution)/shard_map/while/body/eval_jaxpr/hqk,khd->hqd/dot_general | solution.py:118
  225.5 3.6 %fusion.70 = f32[4,1024,64]{1,2,0:T(8,128)S(1)} fusion(f32[4,512,1024]{2,1,0:T(8,128)S(1)} %get-tuple-element.368, f32[4,1024]{1,0:T(4,128)S(1)} %max.4, pred[1024,512]{0,1:T(8,128)(4,1)S(1)} %or_and_fusion.2, f32[4,1024,64]{1,2,0:T(8,128)S(1)} %get-tuple-element.440, f32[4,1024]{1,0:T(4,128)S(1)} %get-tuple-element.370, ...), kind=kOutput, calls=%fused_computation.29.clone.1 | convolution fusion | flops 279445504 | bytes 11305472 | tf_op jit(solution)/shard_map/while/body/eval_jaxpr/hqk,khd->hqd/dot_general | solution.py:118
  234.5 3.6 %fusion.70 = f32[4,1024,64]{1,2,0:T(8,128)S(1)} fusion(f32[4,512,1024]{2,1,0:T(8,128)S(1)} %get-tuple-element.368, f32[4,1024]{1,0:T(4,128)S(1)} %max.4, pred[1024,512]{0,1:T(8,128)(4,1)S(1)} %or_and_fusion.2, f32[4,1024,64]{1,2,0:T(8,128)S(1)} %get-tuple-element.440, f32[4,1024]{1,0:T(4,128)S(1)} %get-tuple-element.370, ...), kind=kOutput, calls=%fused_computation.29.clone.1 | convolution fusion | flops 279445504 | bytes 11305472 | tf_op jit(solution)/shard_map/while/body/eval_jaxpr/hqk,khd->hqd/dot_general | solution.py:118
  243.6 3.6 %fusion.70 = f32[4,1024,64]{1,2,0:T(8,128)S(1)} fusion(f32[4,512,1024]{2,1,0:T(8,128)S(1)} %get-tuple-element.368, f32[4,1024]{1,0:T(4,128)S(1)} %max.4, pred[1024,512]{0,1:T(8,128)(4,1)S(1)} %or_and_fusion.2, f32[4,1024,64]{1,2,0:T(8,128)S(1)} %get-tuple-element.440, f32[4,1024]{1,0:T(4,128)S(1)} %get-tuple-element.370, ...), kind=kOutput, calls=%fused_computation.29.clone.1 | convolution fusion | flops 279445504 | bytes 11305472 | tf_op jit(solution)/shard_map/while/body/eval_jaxpr/hqk,khd->hqd/dot_general | solution.py:118
  252.7 3.6 %fusion.70 = f32[4,1024,64]{1,2,0:T(8,128)S(1)} fusion(f32[4,512,1024]{2,1,0:T(8,128)S(1)} %get-tuple-element.368, f32[4,1024]{1,0:T(4,128)S(1)} %max.4, pred[1024,512]{0,1:T(8,128)(4,1)S(1)} %or_and_fusion.2, f32[4,1024,64]{1,2,0:T(8,128)S(1)} %get-tuple-element.440, f32[4,1024]{1,0:T(4,128)S(1)} %get-tuple-element.370, ...), kind=kOutput, calls=%fused_computation.29.clone.1 | convolution fusion | flops 279445504 | bytes 11305472 | tf_op jit(solution)/shard_map/while/body/eval_jaxpr/hqk,khd->hqd/dot_general | solution.py:118
  261.7 3.6 %fusion.70 = f32[4,1024,64]{1,2,0:T(8,128)S(1)} fusion(f32[4,512,1024]{2,1,0:T(8,128)S(1)} %get-tuple-element.368, f32[4,1024]{1,0:T(4,128)S(1)} %max.4, pred[1024,512]{0,1:T(8,128)(4,1)S(1)} %or_and_fusion.2, f32[4,1024,64]{1,2,0:T(8,128)S(1)} %get-tuple-element.440, f32[4,1024]{1,0:T(4,128)S(1)} %get-tuple-element.370, ...), kind=kOutput, calls=%fused_computation.29.clone.1 | convolution fusion | flops 279445504 | bytes 11305472 | tf_op jit(solution)/shard_map/while/body/eval_jaxpr/hqk,khd->hqd/dot_general | solution.py:118
  270.8 3.6 %fusion.70 = f32[4,1024,64]{1,2,0:T(8,128)S(1)} fusion(f32[4,512,1024]{2,1,0:T(8,128)S(1)} %get-tuple-element.368, f32[4,1024]{1,0:T(4,128)S(1)} %max.4, pred[1024,512]{0,1:T(8,128)(4,1)S(1)} %or_and_fusion.2, f32[4,1024,64]{1,2,0:T(8,128)S(1)} %get-tuple-element.440, f32[4,1024]{1,0:T(4,128)S(1)} %get-tuple-element.370, ...), kind=kOutput, calls=%fused_computation.29.clone.1 | convolution fusion | flops 279445504 | bytes 11305472 | tf_op jit(solution)/shard_map/while/body/eval_jaxpr/hqk,khd->hqd/dot_general | solution.py:118
  298.0 3.6 %fusion.70 = f32[4,1024,64]{1,2,0:T(8,128)S(1)} fusion(f32[4,512,1024]{2,1,0:T(8,128)S(1)} %get-tuple-element.368, f32[4,1024]{1,0:T(4,128)S(1)} %max.4, pred[1024,512]{0,1:T(8,128)(4,1)S(1)} %or_and_fusion.2, f32[4,1024,64]{1,2,0:T(8,128)S(1)} %get-tuple-element.440, f32[4,1024]{1,0:T(4,128)S(1)} %get-tuple-element.370, ...), kind=kOutput, calls=%fused_computation.29.clone.1 | convolution fusion | flops 279445504 | bytes 11305472 | tf_op jit(solution)/shard_map/while/body/eval_jaxpr/hqk,khd->hqd/dot_general | solution.py:118
  303.9 29.2 %reduce-scatter.2.cloned.1.call-done = bf16[256,1024]{1,0:T(8,128)(2,1)} async-done(((bf16[1024,1024]{1,0:T(8,128)(2,1)}), bf16[256,1024]{1,0:T(8,128)(2,1)}) %reduce-scatter.2.cloned.1.call-update) | async-done | bytes 524304 | tf_op jit(solution)/shard_map/reduce_scatter | solution.py:132
  (179 shorter events, 129.7 us)
Async XLA Ops:
  6.5 295.2 %copy-start = (bf16[256,1024]{1,0:T(8,128)(2,1)S(1)}, bf16[256,1024]{1,0:T(8,128)(2,1)}, u32[]{:S(2)}) copy-start(bf16[256,1024]{1,0:T(8,128)(2,1)} %param.17) | copy-start | bytes 1572868
  6.5 37.5 %all-gather.3.cloned.1.call-start = ((), (), s32[]{:S(2)}) async-start(), calls=%async_computation.1 | async-start | bytes 2621440 | tf_op jit(solution)/shard_map/all_gather | solution.py:41
  9.9 89.7 %all-gather.5.cloned.1.call-start = ((), (), s32[]{:S(2)}) async-start(), calls=%async_computation.2 | async-start | bytes 8650752 | tf_op jit(solution)/shard_map/all_gather | solution.py:91
  10.6 322.5 %reduce-scatter.2.cloned.1.call-start = ((), (), s32[]{:S(2)}) async-start(), calls=%async_computation.3 | async-start | bytes 2621440 | tf_op jit(solution)/shard_map/reduce_scatter | solution.py:132
  10.7 37.7 %copy-start.1 = (s32[1,1024]{1,0:T(1,128)S(1)}, s32[1,1024]{1,0:T(1,128)}, u32[]{:S(2)}) copy-start(s32[1,1024]{1,0:T(1,128)} %param.22) | copy-start | bytes 12292
Sparse Core Ops, SparseCore 0:
  10.0 34.0 all-gather.2
  46.4 53.0 all-gather.4
  304.0 29.0 reduce-scatter.1
where the time goes:
time: 342 us; the launch traced here: 340 us
  matrix products  116 us (34%)
  waiting for transfers between devices  84.7 us (25%)
  local copies, waits for them, and re-layouts  63.5 us (19%)
  other arithmetic  57.9 us (17%)
  between operations  13.2 us (4%)
  loops' own time  4.56 us (1%)
    dot_general x16, matrix products, one_step(): jnp.einsum('hqk,khd->hqd', weights.astype(jnp.bfloat16), value_block, pre...  58.4 us
    dot_general x16, matrix products, one_step(): jnp.einsum('qhd,khd->hqk', queries, key_block, preferred_element_type=jnp...  40.8 us
    reduce_sum x16, other arithmetic, one_step(): row_sum = row_sum * rescale + jnp.sum(weights, axis=2)  33.7 us
    reduce_scatter x1, waiting for transfers between devices, shards(): lax.psum_scatter(jnp.dot(attention, w_out, preferred_element_type=jnp.flo...  29.2 us
    all_gather x1, waiting for transfers between devices, shards(): lax.all_gather(normed, 'head', axis=0, tiled=True)  27.6 us
    all_gather x1, waiting for transfers between devices, shards(): shard_piece = lax.all_gather(cache_kv, 'page', axis=1, tiled=True)  27.1 us
    while x2, local copies, waits for them, and re-layouts, shards(): lax.scan(one_step, initial, (key_blocks, value_blocks, key_nodes, key_val...  25.4 us
    another operation x1, local copies, waits for them, and re-layouts, shards(): shard_piece[0].reshape(step_count, block_keys, group_heads, head_size)  12.9 us
  transfers between devices with their start and end apart: 3, of which 3 were waited for; matrix products, arithmetic and copies ran while one was open for 9% of the time, Pallas kernels for 0%

commit v1 on v0

--- a/solution.py
+++ b/solution.py
@@ -38,7 +38,9 @@
     group_heads = group_width // head_size
     weight_flat = w_qkv.reshape(model_width, 3 * group_width)
     projected = jnp.dot(
-        lax.all_gather(normed, "head", axis=0, tiled=True),
+        jnp.concatenate(
+            lax.all_to_all(jnp.stack([normed] * lax.axis_size("head")), "head", 0, 0), axis=0
+        ),
         weight_flat,
         preferred_element_type=jnp.float32,
     ).astype(jnp.bfloat16)

time: 342 us -> 317 us (0.927)
  waiting for transfers between devices: 84.7 us -> 53.6 us
  starting transfers between devices: 0.08 us -> 5.88 us
    all_gather x1 -> x0, waiting for transfers between devices: 27.6 us -> none  [shards(): lax.all_gather(normed, 'head', axis=0, tiled=True)]
    all_gather x1, waiting for transfers between devices: 27.1 us -> 0.02 us  [shards(): shard_piece = lax.all_gather(cache_kv, 'page', axis=1, tiled=True)]
    all_to_all x0 -> x1, waiting for transfers between devices: none -> 22.2 us  [shards(): lax.all_to_all(jnp.stack([normed] * lax.axis_size('head')), 'head', 0, 0)]
    all_to_all x0 -> x1, starting transfers between devices: none -> 5.84 us  [shards(): lax.all_to_all(jnp.stack([normed] * lax.axis_size('head')), 'head', 0, 0)]
  transfers between devices with their start and end apart: 3 -> 3, of which waited for: 3 -> 2; matrix products, arithmetic and copies ran while one was open for 9% -> 11% of each run, Pallas kernels for 0% -> 0%
where the time goes in v1:
time: 317 us; the launch traced here: 314 us
  matrix products  116 us (37%)
  local copies, waits for them, and re-layouts  66 us (21%)
  other arithmetic  55 us (17%)
  waiting for transfers between devices  53.6 us (17%)
  between operations  13.6 us (4%)
  starting transfers between devices  5.88 us (2%)
  loops' own time  4.61 us (1%)
    dot_general x16, matrix products, one_step(): jnp.einsum('hqk,khd->hqd', weights.astype(jnp.bfloat16), value_block, pre...  58.4 us
    dot_general x16, matrix products, one_step(): jnp.einsum('qhd,khd->hqk', queries, key_block, preferred_element_type=jnp...  40.8 us
    reduce_sum x16, other arithmetic, one_step(): row_sum = row_sum * rescale + jnp.sum(weights, axis=2)  33.7 us
    reduce_scatter x1, waiting for transfers between devices, shards(): lax.psum_scatter(jnp.dot(attention, w_out, preferred_element_type=jnp.flo...  30.7 us
    while x2, local copies, waits for them, and re-layouts, shards(): lax.scan(one_step, initial, (key_blocks, value_blocks, key_nodes, key_val...  25.4 us
    all_to_all x1, waiting for transfers between devices, shards(): lax.all_to_all(jnp.stack([normed] * lax.axis_size('head')), 'head', 0, 0)  22.2 us
    another operation x1, local copies, waits for them, and re-layouts, shards(): shard_piece[0].reshape(step_count, block_keys, group_heads, head_size)  12.9 us
    another operation x1, local copies, waits for them, and re-layouts, shards(): shard_piece[1].reshape(step_count, block_keys, group_heads, head_size)  12.9 us
  transfers between devices with their start and end apart: 3, of which 2 were waited for; matrix products, arithmetic and copies ran while one was open for 11% of the time, Pallas kernels for 0%

profile of v1, /device:TPU:1, one launch (start us, length us, event | category | flops | bytes accessed | tf_op | source)
XLA Modules:
  0.0 314.2 jit_solution(2536403732086591634)
XLA Ops:
  11.4 5.8 %all-to-all-start = ((bf16[4,256,1024]{2,1,0:T(8,128)(2,1)}), bf16[4,256,1024]{2,1,0:T(8,128)(2,1)S(1)}, u32[]{:S(2)}, u32[]{:S(2)}) async-start(bf16[4,256,1024]{2,1,0:T(8,128)(2,1)} %stack.10), calls=%async_computation | async-start | bytes 4194304 | tf_op jit(solution)/shard_map/all_to_all | solution.py:42
  20.6 22.2 %all-to-all-done = bf16[4,256,1024]{2,1,0:T(8,128)(2,1)S(1)} async-done(((bf16[4,256,1024]{2,1,0:T(8,128)(2,1)}), bf16[4,256,1024]{2,1,0:T(8,128)(2,1)S(1)}, u32[]{:S(2)}, u32[]{:S(2)}) %all-to-all-start) | async-done | bytes 2097184 | tf_op jit(solution)/shard_map/all_to_all | solution.py:42
  46.9 24.1 %while.30 = (s32[]{:T(128)}, f32[2,4,512]{2,1,0:T(4,128)S(1)}, f32[2,4,512]{2,1,0:T(4,128)S(1)}, f32[2,4,512,64]{2,3,1,0:T(8,128)}, s32[2]{0:T(128)S(1)}, /*inde...) while((s32[]{:T(128)}, f32[2,4,512]{2,1,0:T(4,128)S(1)}, ...), condition=%wide.region_4.5_spmd.clone, body=%wide.region_1.4_spmd.clone.sunk | while | flops 565703168 | bytes 37566712 | solution.py:85
  72.3 6.0 %fusion.44 = (bf16[1,64,128,256]{3,2,1,0:T(8,128)(2,1)}, bf16[1,64,128,256]{3,2,1,0:T(8,128)(2,1)}) fusion(bf16[2,64,128,256]{3,2,1,0:T(8,128)(2,1)} %all-gather.2.cloned.1.call-done), kind=kLoop, calls=%fused_computation.64 | loop fusion | bytes 16777216 | tf_op jit(solution)/shard_map/slice | solution.py:99
  78.3 12.9 %reshape.241 = bf16[16,512,4,64]{3,2,1,0:T(4,128)(2,1)} reshape(bf16[1,64,128,256]{3,2,1,0:T(8,128)(2,1)} %get-tuple-element.231) | data formatting | bytes 8388608 | tf_op jit(solution)/shard_map/reshape;squeeze | solution.py:98
  91.2 12.7 %copy.24 = bf16[16,512,4,64]{1,3,2,0:T(8,128)(2,1)} copy(bf16[16,512,4,64]{3,2,1,0:T(4,128)(2,1)} %reshape.241) | data formatting | bytes 8388608 | tf_op jit(solution)/shard_map/while | solution.py:128
  103.9 12.9 %reshape.242 = bf16[16,512,4,64]{3,2,1,0:T(4,128)(2,1)} reshape(bf16[1,64,128,256]{3,2,1,0:T(8,128)(2,1)} %get-tuple-element.230) | data formatting | bytes 8388608 | tf_op jit(solution)/shard_map/reshape;squeeze | solution.py:99
  116.8 12.7 %copy.25 = bf16[16,512,4,64]{1,3,2,0:T(8,128)(2,1)} copy(bf16[16,512,4,64]{3,2,1,0:T(4,128)(2,1)} %reshape.242) | data formatting | bytes 8388608 | tf_op jit(solution)/shard_map/while | solution.py:128
  129.5 145.0 %while.29 = (s32[]{:T(128)}, f32[4,1024]{1,0:T(4,128)S(1)}, f32[4,1024]{1,0:T(4,128)S(1)}, f32[4,1024,64]{1,2,0:T(8,128)S(1)}, s32[16,512]{1,0:T(8,128)S(1)}, /*...) while((s32[]{:T(128)}, f32[4,1024]{1,0:T(4,128)S(1)}, ...), condition=%wide.region_11.12_spmd, body=%wide.region_8.11_spmd.sunk | while | flops 567812096 | bytes 30691972 | solution.py:128
  134.8 3.6 %fusion.71 = f32[4,1024,64]{1,2,0:T(8,128)S(1)} fusion(f32[4,512,1024]{2,1,0:T(8,128)S(1)} %get-tuple-element.368, f32[4,1024]{1,0:T(4,128)S(1)} %max.4, pred[1024,512]{0,1:T(8,128)(4,1)S(1)} %or_and_fusion.2, f32[4,1024,64]{1,2,0:T(8,128)S(1)} %get-tuple-element.440, f32[4,1024]{1,0:T(4,128)S(1)} %get-tuple-element.370, ...), kind=kOutput, calls=%fused_computation.29.clone.1 | convolution fusion | flops 279445504 | bytes 11305472 | tf_op jit(solution)/shard_map/while/body/eval_jaxpr/hqk,khd->hqd/dot_general | solution.py:120
  143.9 3.6 %fusion.71 = f32[4,1024,64]{1,2,0:T(8,128)S(1)} fusion(f32[4,512,1024]{2,1,0:T(8,128)S(1)} %get-tuple-element.368, f32[4,1024]{1,0:T(4,128)S(1)} %max.4, pred[1024,512]{0,1:T(8,128)(4,1)S(1)} %or_and_fusion.2, f32[4,1024,64]{1,2,0:T(8,128)S(1)} %get-tuple-element.440, f32[4,1024]{1,0:T(4,128)S(1)} %get-tuple-element.370, ...), kind=kOutput, calls=%fused_computation.29.clone.1 | convolution fusion | flops 279445504 | bytes 11305472 | tf_op jit(solution)/shard_map/while/body/eval_jaxpr/hqk,khd->hqd/dot_general | solution.py:120
  153.0 3.6 %fusion.71 = f32[4,1024,64]{1,2,0:T(8,128)S(1)} fusion(f32[4,512,1024]{2,1,0:T(8,128)S(1)} %get-tuple-element.368, f32[4,1024]{1,0:T(4,128)S(1)} %max.4, pred[1024,512]{0,1:T(8,128)(4,1)S(1)} %or_and_fusion.2, f32[4,1024,64]{1,2,0:T(8,128)S(1)} %get-tuple-element.440, f32[4,1024]{1,0:T(4,128)S(1)} %get-tuple-element.370, ...), kind=kOutput, calls=%fused_computation.29.clone.1 | convolution fusion | flops 279445504 | bytes 11305472 | tf_op jit(solution)/shard_map/while/body/eval_jaxpr/hqk,khd->hqd/dot_general | solution.py:120
  162.0 3.6 %fusion.71 = f32[4,1024,64]{1,2,0:T(8,128)S(1)} fusion(f32[4,512,1024]{2,1,0:T(8,128)S(1)} %get-tuple-element.368, f32[4,1024]{1,0:T(4,128)S(1)} %max.4, pred[1024,512]{0,1:T(8,128)(4,1)S(1)} %or_and_fusion.2, f32[4,1024,64]{1,2,0:T(8,128)S(1)} %get-tuple-element.440, f32[4,1024]{1,0:T(4,128)S(1)} %get-tuple-element.370, ...), kind=kOutput, calls=%fused_computation.29.clone.1 | convolution fusion | flops 279445504 | bytes 11305472 | tf_op jit(solution)/shard_map/while/body/eval_jaxpr/hqk,khd->hqd/dot_general | solution.py:120
  171.1 3.6 %fusion.71 = f32[4,1024,64]{1,2,0:T(8,128)S(1)} fusion(f32[4,512,1024]{2,1,0:T(8,128)S(1)} %get-tuple-element.368, f32[4,1024]{1,0:T(4,128)S(1)} %max.4, pred[1024,512]{0,1:T(8,128)(4,1)S(1)} %or_and_fusion.2, f32[4,1024,64]{1,2,0:T(8,128)S(1)} %get-tuple-element.440, f32[4,1024]{1,0:T(4,128)S(1)} %get-tuple-element.370, ...), kind=kOutput, calls=%fused_computation.29.clone.1 | convolution fusion | flops 279445504 | bytes 11305472 | tf_op jit(solution)/shard_map/while/body/eval_jaxpr/hqk,khd->hqd/dot_general | solution.py:120
  180.2 3.6 %fusion.71 = f32[4,1024,64]{1,2,0:T(8,128)S(1)} fusion(f32[4,512,1024]{2,1,0:T(8,128)S(1)} %get-tuple-element.368, f32[4,1024]{1,0:T(4,128)S(1)} %max.4, pred[1024,512]{0,1:T(8,128)(4,1)S(1)} %or_and_fusion.2, f32[4,1024,64]{1,2,0:T(8,128)S(1)} %get-tuple-element.440, f32[4,1024]{1,0:T(4,128)S(1)} %get-tuple-element.370, ...), kind=kOutput, calls=%fused_computation.29.clone.1 | convolution fusion | flops 279445504 | bytes 11305472 | tf_op jit(solution)/shard_map/while/body/eval_jaxpr/hqk,khd->hqd/dot_general | solution.py:120
  189.2 3.6 %fusion.71 = f32[4,1024,64]{1,2,0:T(8,128)S(1)} fusion(f32[4,512,1024]{2,1,0:T(8,128)S(1)} %get-tuple-element.368, f32[4,1024]{1,0:T(4,128)S(1)} %max.4, pred[1024,512]{0,1:T(8,128)(4,1)S(1)} %or_and_fusion.2, f32[4,1024,64]{1,2,0:T(8,128)S(1)} %get-tuple-element.440, f32[4,1024]{1,0:T(4,128)S(1)} %get-tuple-element.370, ...), kind=kOutput, calls=%fused_computation.29.clone.1 | convolution fusion | flops 279445504 | bytes 11305472 | tf_op jit(solution)/shard_map/while/body/eval_jaxpr/hqk,khd->hqd/dot_general | solution.py:120
  198.3 3.6 %fusion.71 = f32[4,1024,64]{1,2,0:T(8,128)S(1)} fusion(f32[4,512,1024]{2,1,0:T(8,128)S(1)} %get-tuple-element.368, f32[4,1024]{1,0:T(4,128)S(1)} %max.4, pred[1024,512]{0,1:T(8,128)(4,1)S(1)} %or_and_fusion.2, f32[4,1024,64]{1,2,0:T(8,128)S(1)} %get-tuple-element.440, f32[4,1024]{1,0:T(4,128)S(1)} %get-tuple-element.370, ...), kind=kOutput, calls=%fused_computation.29.clone.1 | convolution fusion | flops 279445504 | bytes 11305472 | tf_op jit(solution)/shard_map/while/body/eval_jaxpr/hqk,khd->hqd/dot_general | solution.py:120
  207.3 3.6 %fusion.71 = f32[4,1024,64]{1,2,0:T(8,128)S(1)} fusion(f32[4,512,1024]{2,1,0:T(8,128)S(1)} %get-tuple-element.368, f32[4,1024]{1,0:T(4,128)S(1)} %max.4, pred[1024,512]{0,1:T(8,128)(4,1)S(1)} %or_and_fusion.2, f32[4,1024,64]{1,2,0:T(8,128)S(1)} %get-tuple-element.440, f32[4,1024]{1,0:T(4,128)S(1)} %get-tuple-element.370, ...), kind=kOutput, calls=%fused_computation.29.clone.1 | convolution fusion | flops 279445504 | bytes 11305472 | tf_op jit(solution)/shard_map/while/body/eval_jaxpr/hqk,khd->hqd/dot_general | solution.py:120
  216.4 3.6 %fusion.71 = f32[4,1024,64]{1,2,0:T(8,128)S(1)} fusion(f32[4,512,1024]{2,1,0:T(8,128)S(1)} %get-tuple-element.368, f32[4,1024]{1,0:T(4,128)S(1)} %max.4, pred[1024,512]{0,1:T(8,128)(4,1)S(1)} %or_and_fusion.2, f32[4,1024,64]{1,2,0:T(8,128)S(1)} %get-tuple-element.440, f32[4,1024]{1,0:T(4,128)S(1)} %get-tuple-element.370, ...), kind=kOutput, calls=%fused_computation.29.clone.1 | convolution fusion | flops 279445504 | bytes 11305472 | tf_op jit(solution)/shard_map/while/body/eval_jaxpr/hqk,khd->hqd/dot_general | solution.py:120
  225.5 3.6 %fusion.71 = f32[4,1024,64]{1,2,0:T(8,128)S(1)} fusion(f32[4,512,1024]{2,1,0:T(8,128)S(1)} %get-tuple-element.368, f32[4,1024]{1,0:T(4,128)S(1)} %max.4, pred[1024,512]{0,1:T(8,128)(4,1)S(1)} %or_and_fusion.2, f32[4,1024,64]{1,2,0:T(8,128)S(1)} %get-tuple-element.440, f32[4,1024]{1,0:T(4,128)S(1)} %get-tuple-element.370, ...), kind=kOutput, calls=%fused_computation.29.clone.1 | convolution fusion | flops 279445504 | bytes 11305472 | tf_op jit(solution)/shard_map/while/body/eval_jaxpr/hqk,khd->hqd/dot_general | solution.py:120
  234.5 3.6 %fusion.71 = f32[4,1024,64]{1,2,0:T(8,128)S(1)} fusion(f32[4,512,1024]{2,1,0:T(8,128)S(1)} %get-tuple-element.368, f32[4,1024]{1,0:T(4,128)S(1)} %max.4, pred[1024,512]{0,1:T(8,128)(4,1)S(1)} %or_and_fusion.2, f32[4,1024,64]{1,2,0:T(8,128)S(1)} %get-tuple-element.440, f32[4,1024]{1,0:T(4,128)S(1)} %get-tuple-element.370, ...), kind=kOutput, calls=%fused_computation.29.clone.1 | convolution fusion | flops 279445504 | bytes 11305472 | tf_op jit(solution)/shard_map/while/body/eval_jaxpr/hqk,khd->hqd/dot_general | solution.py:120
  243.6 3.6 %fusion.71 = f32[4,1024,64]{1,2,0:T(8,128)S(1)} fusion(f32[4,512,1024]{2,1,0:T(8,128)S(1)} %get-tuple-element.368, f32[4,1024]{1,0:T(4,128)S(1)} %max.4, pred[1024,512]{0,1:T(8,128)(4,1)S(1)} %or_and_fusion.2, f32[4,1024,64]{1,2,0:T(8,128)S(1)} %get-tuple-element.440, f32[4,1024]{1,0:T(4,128)S(1)} %get-tuple-element.370, ...), kind=kOutput, calls=%fused_computation.29.clone.1 | convolution fusion | flops 279445504 | bytes 11305472 | tf_op jit(solution)/shard_map/while/body/eval_jaxpr/hqk,khd->hqd/dot_general | solution.py:120
  270.8 3.6 %fusion.71 = f32[4,1024,64]{1,2,0:T(8,128)S(1)} fusion(f32[4,512,1024]{2,1,0:T(8,128)S(1)} %get-tuple-element.368, f32[4,1024]{1,0:T(4,128)S(1)} %max.4, pred[1024,512]{0,1:T(8,128)(4,1)S(1)} %or_and_fusion.2, f32[4,1024,64]{1,2,0:T(8,128)S(1)} %get-tuple-element.440, f32[4,1024]{1,0:T(4,128)S(1)} %get-tuple-element.370, ...), kind=kOutput, calls=%fused_computation.29.clone.1 | convolution fusion | flops 279445504 | bytes 11305472 | tf_op jit(solution)/shard_map/while/body/eval_jaxpr/hqk,khd->hqd/dot_general | solution.py:120
  276.7 30.7 %reduce-scatter.2.cloned.1.call-done = bf16[256,1024]{1,0:T(8,128)(2,1)} async-done(((bf16[1024,1024]{1,0:T(8,128)(2,1)}), bf16[256,1024]{1,0:T(8,128)(2,1)}) %reduce-scatter.2.cloned.1.call-update) | async-done | bytes 524304 | tf_op jit(solution)/shard_map/reduce_scatter | solution.py:134
  (195 shorter events, 129.1 us)
Async XLA Ops:
  6.5 268.0 %copy-start = (bf16[256,1024]{1,0:T(8,128)(2,1)S(1)}, bf16[256,1024]{1,0:T(8,128)(2,1)}, u32[]{:S(2)}) copy-start(bf16[256,1024]{1,0:T(8,128)(2,1)} %param.17) | copy-start | bytes 1572868
  6.5 13.3 %copy-start.5 = (s32[64]{0:T(128)S(1)}, s32[64]{0:T(128)}, u32[]{:S(2)}) copy-start(s32[64]{0:T(128)} %param.19) | copy-start | bytes 772
  6.5 13.5 %copy-start.6 = (s32[64]{0:T(128)S(1)}, s32[64]{0:T(128)}, u32[]{:S(2)}) copy-start(s32[64]{0:T(128)} %param.20) | copy-start | bytes 772
  6.5 13.6 %copy-start.3 = (s32[1,1024]{1,0:T(1,128)S(1)}, s32[1,1024]{1,0:T(1,128)}, u32[]{:S(2)}) copy-start(s32[1,1024]{1,0:T(1,128)} %param.22) | copy-start | bytes 12292
  6.5 13.6 %copy-start.7 = (s32[1,8]{1,0:T(1,128)S(1)}, s32[1,8]{1,0:T(1,128)}, u32[]{:S(2)}) copy-start(s32[1,8]{1,0:T(1,128)} %param.23) | copy-start | bytes 100
  6.5 13.7 %copy-start.4 = (s32[19]{0:T(128)S(1)}, s32[19]{0:T(128)}, u32[]{:S(2)}) copy-start(s32[19]{0:T(128)} %param.21) | copy-start | bytes 232
  6.6 65.8 %all-gather.2.cloned.1.call-start = ((), (), s32[]{:S(2)}) async-start(), calls=%async_computation.2 | async-start | bytes 8650752 | tf_op jit(solution)/shard_map/all_gather | solution.py:93
  11.4 31.3 %all-to-all-start = ((bf16[4,256,1024]{2,1,0:T(8,128)(2,1)}), bf16[4,256,1024]{2,1,0:T(8,128)(2,1)S(1)}, u32[]{:S(2)}, u32[]{:S(2)}) async-start(bf16[4,256,1024]{2,1,0:T(8,128)(2,1)} %stack.10), calls=%async_computation | async-start | bytes 4194304 | tf_op jit(solution)/shard_map/all_to_all | solution.py:42
  17.3 290.1 %reduce-scatter.2.cloned.1.call-start = ((), (), s32[]{:S(2)}) async-start(), calls=%async_computation.3 | async-start | bytes 2621440 | tf_op jit(solution)/shard_map/reduce_scatter | solution.py:134
  46.9 5.5 %copy-start.1 = (f32[2,4,512,64]{2,3,1,0:T(8,128)S(1)}, f32[2,4,512,64]{2,3,1,0:T(8,128)}, u32[]{:S(2)}) copy-start(f32[2,4,512,64]{2,3,1,0:T(8,128)} %get-tuple-element.401) | copy-start | bytes 3145732 | tf_op jit(solution)/shard_map/while
  56.0 2.9 copy-start.2
  58.9 5.5 %copy-start.1 = (f32[2,4,512,64]{2,3,1,0:T(8,128)S(1)}, f32[2,4,512,64]{2,3,1,0:T(8,128)}, u32[]{:S(2)}) copy-start(f32[2,4,512,64]{2,3,1,0:T(8,128)} %get-tuple-element.401) | copy-start | bytes 3145732 | tf_op jit(solution)/shard_map/while
  68.0 2.9 copy-start.2
Sparse Core Ops, SparseCore 0:
  9.7 56.2 all-gather.1
  276.8 30.5 reduce-scatter.1
